TPU v7x, 128 devices: a whole 4x4x4 slice. The times are simulated.
128 devices in a mesh: grp: 8 (over z, core), dev: 16 (over y, x).
Axes of the slice: x: 4, y: 4, z: 4, core: 2. Of those that a mesh axis runs over, the one named last changes fastest.
Arguments:
- positions: float32 [3, 131072], P(None, ('grp', 'dev')), may hold values from -3 to 3
- velocities: float32 [3, 131072], P(None, ('grp', 'dev')), may hold values from -5 to 5
- accelerations: float32 [3, 131072], P(None, ('grp', 'dev')), may hold values from -3 to 3
- jerks: float32 [3, 131072], P(None, ('grp', 'dev')), may hold values from -3 to 3
- levels: int32 [131072], P(('grp', 'dev')), may hold values from 0 to 5
- counts: int32 [2, 128], replicated, may hold values from 1 to 256, 16384 in all within a row
- active_rows: int32 [2, 32768], P(None, ('grp', 'dev')), may hold values from 0 to 1023, as said below
Outputs:
- new_positions: float32 [3, 131072], P(None, ('grp', 'dev'))
- new_velocities: float32 [3, 131072], P(None, ('grp', 'dev'))
- new_accelerations: float32 [3, 131072], P(None, ('grp', 'dev'))
- new_jerks: float32 [3, 131072], P(None, ('grp', 'dev'))
Inputs may be any that keep to these rules, and one draw needn't show every extreme that they name: In each step the 128 counts sum to exactly 16384 and the largest of them is exactly 256. `active_rows`: for each step and device, the 256 entries of the device's slots are distinct indices of that device's own stars; only the first counts of them are live.
All inputs are finite; a program needn't handle non-finite values.
Results may differ from a plain program's by a relative error of at most 0.00022.
Values sent between devices are 32-bit elements; how exact they have to be, the bound alone decides.
No kernel may reach another device: no remote copies, remote signals or barrier semaphores. Data moves between devices by JAX's collectives and lax.ppermute only.
A program may use at most 128 MiB of HBM per device.

v0:
```python
import math
import jax
import jax.numpy as jnp
from jax import lax
from jax.sharding import PartitionSpec as P

tick_length = 1.0 / 128.0


def pair_block(targets, src_pos, src_vel, mass, soft_sq):
    gap_x = src_pos[0][None, :] - targets[0][:, None]
    gap_y = src_pos[1][None, :] - targets[1][:, None]
    gap_z = src_pos[2][None, :] - targets[2][:, None]
    drift_x = src_vel[0][None, :] - targets[3][:, None]
    drift_y = src_vel[1][None, :] - targets[4][:, None]
    drift_z = src_vel[2][None, :] - targets[5][:, None]
    squared = gap_x * gap_x + gap_y * gap_y + gap_z * gap_z + soft_sq
    inverse = lax.rsqrt(squared)
    weight = mass * inverse * inverse * inverse
    along = 3.0 * (gap_x * drift_x + gap_y * drift_y + gap_z * drift_z) * inverse * inverse
    return jnp.stack(
        [
            jnp.sum(weight * gap_x, axis=1),
            jnp.sum(weight * gap_y, axis=1),
            jnp.sum(weight * gap_z, axis=1),
            jnp.sum(weight * (drift_x - along * gap_x), axis=1),
            jnp.sum(weight * (drift_y - along * gap_y), axis=1),
            jnp.sum(weight * (drift_z - along * gap_z), axis=1),
        ]
    )


def block_terms(packed, src_pos, src_vel, mass, soft_sq):
    width, total = packed.shape
    block = math.gcd(total, 2048)
    grouped = packed.reshape(width, total // block, block).transpose(1, 0, 2)
    result = lax.map(lambda targets: pair_block(targets, src_pos, src_vel, mass, soft_sq), grouped)
    return result.transpose(1, 0, 2).reshape(width, total)


def predict(positions, velocities, accelerations, jerks, elapsed):
    span = elapsed[None, :]
    pred_pos = (
        positions
        + span * velocities
        + 0.5 * span * span * accelerations
        + span * span * span / 6.0 * jerks
    )
    pred_vel = velocities + span * accelerations + 0.5 * span * span * jerks
    return (pred_pos, pred_vel)


def correct(old_pos, old_vel, old_acc, old_jerk, force, jerk_new, span):
    span = span[None, :]
    new_vel = old_vel + 0.5 * span * (old_acc + force) + span * span / 12.0 * (old_jerk - jerk_new)
    new_pos = old_pos + 0.5 * span * (old_vel + new_vel) + span * span / 12.0 * (old_acc - force)
    return (new_pos, new_vel)


def shards(positions, velocities, accelerations, jerks, levels, counts, active_rows):
    devices_all = lax.axis_size("grp") * lax.axis_size("dev")
    my_rank = lax.axis_index("grp") * lax.axis_size("dev") + lax.axis_index("dev")
    star_dev = positions.shape[1]
    slot_cap = active_rows.shape[1]
    stars_all = star_dev * devices_all
    live_all = stars_all // 8
    mass = 1.0 / stars_all
    soft_sq = 0.0004 * (131072.0 / stars_all) ** (2.0 / 3.0)
    chunks = 4
    chunk = live_all // chunks
    last_time = -(jnp.left_shift(jnp.int32(1), levels) - 1).astype(jnp.float32) * tick_length
    for step in range(active_rows.shape[0]):
        now = (step + 1) * tick_length
        pred_pos, pred_vel = predict(positions, velocities, accelerations, jerks, now - last_time)
        rows = active_rows[step]
        targets = jnp.concatenate([pred_pos[:, rows], pred_vel[:, rows]], axis=0)
        step_counts = counts[step]
        own_count = step_counts[my_rank]
        inclusive = jnp.cumsum(step_counts).astype(jnp.int32)
        first = inclusive - step_counts
        place = jnp.arange(live_all, dtype=jnp.int32)
        owner = jnp.sum((inclusive[None, :] <= place[:, None]).astype(jnp.int32), axis=1)
        owner = jnp.minimum(owner, devices_all - 1)
        slot = owner * slot_cap + place - first[owner]
        gathered = lax.all_gather(targets[None], ("grp", "dev"), axis=0, tiled=True)
        flat = gathered.transpose(1, 0, 2).reshape(6, devices_all * slot_cap)
        compact = flat[:, slot]
        parts = []
        summed = None
        for c in range(chunks):
            piece = compact[:, c * chunk : (c + 1) * chunk]
            terms = block_terms(piece, pred_pos, pred_vel, mass, soft_sq)
            if summed is not None:
                terms, summed = lax.optimization_barrier((terms, summed))
                parts.append(summed)
            summed = lax.psum(terms, ("grp", "dev"))
        parts.append(summed)
        parts.append(jnp.zeros((6, slot_cap), jnp.float32))
        totals = jnp.concatenate(parts, axis=1)
        own = lax.dynamic_slice_in_dim(totals, first[my_rank], slot_cap, 1)
        span = now - last_time[rows]
        new_pos, new_vel = correct(
            positions[:, rows],
            velocities[:, rows],
            accelerations[:, rows],
            jerks[:, rows],
            own[:3],
            own[3:],
            span,
        )
        live = jnp.arange(slot_cap, dtype=jnp.int32) < own_count
        target = jnp.where(live, rows, star_dev)
        positions = positions.at[:, target].set(new_pos, mode="drop")
        velocities = velocities.at[:, target].set(new_vel, mode="drop")
        accelerations = accelerations.at[:, target].set(own[:3], mode="drop")
        jerks = jerks.at[:, target].set(own[3:], mode="drop")
        last_time = last_time.at[target].set(now, mode="drop")
    return (positions, velocities, accelerations, jerks)


def solution(mesh):
    placed = (
        P(None, ("grp", "dev")),
        P(None, ("grp", "dev")),
        P(None, ("grp", "dev")),
        P(None, ("grp", "dev")),
        P(("grp", "dev")),
        P(),
        P(None, ("grp", "dev")),
    )
    return jax.shard_map(
        shards,
        mesh=mesh,
        in_specs=placed,
        out_specs=(
            P(None, ("grp", "dev")),
            P(None, ("grp", "dev")),
            P(None, ("grp", "dev")),
            P(None, ("grp", "dev")),
        ),
        check_vma=False,
    )
```

profile of v0, /device:TPU:1, one launch (start us, length us, event | category | flops | bytes accessed | tf_op | source)
XLA Modules:
  0.0 1731.8 jit_solution(9103468403013295511)
XLA Ops:
  14.8 63.9 %all-gather.2 = f32[128,6,256]{2,1,0:T(8,128)S(1)} all-gather(f32[1,6,256]{2,1,0:T(8,128)S(1)} %maximum_bitcast_fusion), channel_id=2, replica_groups=mesh['grp'=8,'dev'=16] {'grp','dev'}, dimensions={0}, use_global_device_ids=true | all-gather | bytes 792576 | tf_op jit(solution)/shard_map/all_gather | solution.py:85
  90.3 97.2 %gather_fusion.6 = s32[16384]{0:T(1024)S(1)} fusion(s32[128]{0:T(128)S(1)} %get-tuple-element.734, s32[16384]{0:T(1024)S(1)} %broadcast_clamp_fusion.3), kind=kCustom, calls=%fused_computation.6 | custom fusion | bytes 196608 | tf_op jit(solution)/shard_map/gather | solution.py:84
  187.7 60.2 %gather_fusion.7 = f32[16384,6]{1,0:T(8,128)} fusion(f32[6,32768]{0,1:T(8,128)} %bitcast.632, s32[16384]{0:T(1024)S(1)} %broadcast_clamp_fusion.1), kind=kCustom, calls=%fused_computation.7 | custom fusion | bytes 851968 | tf_op jit(solution)/shard_map/gather | solution.py:87
  256.3 32.8 %while.81 = (s32[]{:T(128)}, f32[2,6,2048]{2,1,0:T(8,128)S(1)}, f32[3,1024]{1,0:T(4,128)S(1)}, f32[2,6,2048]{2,1,0:T(8,128)S(1)}, f32[3,1024]{1,0:T(4,128)S(1)},...) while((s32[]{:T(128)}, f32[2,6,2048]{2,1,0:T(8,128)S(1)}, ...), condition=%wide.region_17.18_spmd, body=%wide.region_10.17_spmd.sunk | while | flops 85970952 | bytes 499925 | solution.py:37
  256.4 16.2 fusion.187
  272.8 16.2 fusion.187
  294.7 32.8 %while.80 = (s32[]{:T(128)}, f32[2,6,2048]{2,1,0:T(8,128)S(1)}, f32[3,1024]{1,0:T(4,128)S(1)}, f32[2,6,2048]{2,1,0:T(8,128)S(1)}, f32[3,1024]{1,0:T(4,128)S(1)},...) while((s32[]{:T(128)}, f32[2,6,2048]{2,1,0:T(8,128)S(1)}, ...), condition=%wide.region_9.10_spmd, body=%wide.region_2.9_spmd.sunk | while | flops 85970952 | bytes 499925 | solution.py:37
  294.8 16.2 fusion.185
  311.2 16.2 fusion.185
  329.8 32.8 %while.82 = (s32[]{:T(128)}, f32[2,6,2048]{2,1,0:T(8,128)S(1)}, f32[3,1024]{1,0:T(4,128)S(1)}, f32[2,6,2048]{2,1,0:T(8,128)S(1)}, f32[3,1024]{1,0:T(4,128)S(1)},...) while((s32[]{:T(128)}, f32[2,6,2048]{2,1,0:T(8,128)S(1)}, ...), condition=%wide.region_26.27_spmd, body=%wide.region_19.26_spmd.sunk | while | flops 85970952 | bytes 499925 | solution.py:37
  329.9 16.2 fusion.189
  346.4 16.2 fusion.189
  363.3 32.9 %while.83 = (s32[]{:T(128)}, f32[2,6,2048]{2,1,0:T(8,128)S(1)}, f32[3,1024]{1,0:T(4,128)S(1)}, f32[2,6,2048]{2,1,0:T(8,128)S(1)}, f32[3,1024]{1,0:T(4,128)S(1)},...) while((s32[]{:T(128)}, f32[2,6,2048]{2,1,0:T(8,128)S(1)}, ...), condition=%wide.region_35.36_spmd, body=%wide.region_28.35_spmd.sunk | while | flops 85970952 | bytes 499925 | solution.py:37
  363.4 16.2 fusion.191
  379.9 16.2 fusion.191
  399.8 97.2 %gather_fusion.15 = s32[16384]{0:T(1024)S(1)} fusion(s32[128]{0:T(128)S(1)} %get-tuple-element.733, s32[16384]{0:T(1024)S(1)} %broadcast_clamp_fusion.2), kind=kCustom, calls=%fused_computation.15 | custom fusion | bytes 196608 | tf_op jit(solution)/shard_map/gather | solution.py:84
  509.3 137.8 %all-reduce.11.cloned.1.call-done = f32[6,4096]{1,0:T(8,128)} async-done(((f32[6,4096]{1,0:T(8,128)}), f32[6,4096]{1,0:T(8,128)}) %all-reduce.11.cloned.1.call-update) | async-done | bytes 98320 | tf_op jit(solution)/shard_map/psum | solution.py:96
  648.1 141.3 %all-reduce.13.cloned.1.call-done = f32[6,4096]{1,0:T(8,128)} async-done(((f32[6,4096]{1,0:T(8,128)}), f32[6,4096]{1,0:T(8,128)}) %all-reduce.13.cloned.1.call-update) | async-done | bytes 98320 | tf_op jit(solution)/shard_map/psum | solution.py:96
  790.4 141.8 %all-reduce.15.cloned.1.call-done = f32[6,4096]{1,0:T(8,128)} async-done(((f32[6,4096]{1,0:T(8,128)}), f32[6,4096]{1,0:T(8,128)}) %all-reduce.15.cloned.1.call-update) | async-done | bytes 98320 | tf_op jit(solution)/shard_map/psum | solution.py:96
  941.9 59.0 %all-gather.3 = f32[128,6,256]{2,1,0:T(8,128)S(1)} all-gather(f32[1,6,256]{2,1,0:T(8,128)S(1)} %maximum_bitcast_fusion.1), channel_id=3, replica_groups=mesh['grp'=8,'dev'=16] {'grp','dev'}, dimensions={0}, use_global_device_ids=true | all-gather | bytes 792576 | tf_op jit(solution)/shard_map/all_gather | solution.py:85
  1009.3 60.2 %gather_fusion.16 = f32[16384,6]{1,0:T(8,128)} fusion(f32[6,32768]{0,1:T(8,128)} %bitcast.633, s32[16384]{0:T(1024)S(1)} %broadcast_clamp_fusion), kind=kCustom, calls=%fused_computation.16 | custom fusion | bytes 851968 | tf_op jit(solution)/shard_map/gather | solution.py:87
  1077.9 32.8 %while.84 = (s32[]{:T(128)}, f32[2,6,2048]{2,1,0:T(8,128)S(1)}, f32[3,1024]{1,0:T(4,128)S(1)}, f32[2,6,2048]{2,1,0:T(8,128)S(1)}, f32[3,1024]{1,0:T(4,128)S(1)},...) while((s32[]{:T(128)}, f32[2,6,2048]{2,1,0:T(8,128)S(1)}, ...), condition=%wide.region_52.53_spmd, body=%wide.region_45.52_spmd.sunk | while | flops 85970952 | bytes 499925 | solution.py:37
  1113.6 34.0 %while.85 = (s32[]{:T(128)}, f32[2,6,2048]{2,1,0:T(8,128)}, f32[3,1024]{1,0:T(4,128)S(1)}, f32[2,6,2048]{2,1,0:T(8,128)S(1)}, f32[3,1024]{1,0:T(4,128)S(1)}, /*i...) while((s32[]{:T(128)}, f32[2,6,2048]{2,1,0:T(8,128)}, f32[3,1024]{1,0:T(4,128)S(1)}, ...), condition=%wide.region_60.61_spmd, body=%wide.region_53.60_spmd.sunk | while | flops 85970952 | bytes 483541 | solution.py:37
  1113.7 16.2 fusion.195
  1150.1 32.8 %while.86 = (s32[]{:T(128)}, f32[2,6,2048]{2,1,0:T(8,128)S(1)}, f32[3,1024]{1,0:T(4,128)S(1)}, f32[2,6,2048]{2,1,0:T(8,128)S(1)}, f32[3,1024]{1,0:T(4,128)S(1)},...) while((s32[]{:T(128)}, f32[2,6,2048]{2,1,0:T(8,128)S(1)}, ...), condition=%wide.region_69.70_spmd, body=%wide.region_62.69_spmd.sunk | while | flops 85970952 | bytes 499925 | solution.py:37
  1150.2 16.2 fusion.197
  1166.6 16.2 fusion.197
  1183.7 32.8 %while.87 = (s32[]{:T(128)}, f32[2,6,2048]{2,1,0:T(8,128)S(1)}, f32[3,1024]{1,0:T(4,128)S(1)}, f32[2,6,2048]{2,1,0:T(8,128)S(1)}, f32[3,1024]{1,0:T(4,128)S(1)},...) while((s32[]{:T(128)}, f32[2,6,2048]{2,1,0:T(8,128)S(1)}, ...), condition=%wide.region_78.79_spmd, body=%wide.region_71.78_spmd.sunk | while | flops 85970952 | bytes 499925 | solution.py:37
  1219.8 66.7 %all-reduce.17.cloned.1.call-done = f32[6,4096]{1,0:T(8,128)} async-done(((f32[6,4096]{1,0:T(8,128)}), f32[6,4096]{1,0:T(8,128)}) %all-reduce.17.cloned.1.call-update) | async-done | bytes 98320 | tf_op jit(solution)/shard_map/psum | solution.py:96
  1287.5 141.8 %all-reduce.19.cloned.1.call-done = f32[6,4096]{1,0:T(8,128)} async-done(((f32[6,4096]{1,0:T(8,128)}), f32[6,4096]{1,0:T(8,128)}) %all-reduce.19.cloned.1.call-update) | async-done | bytes 98320 | tf_op jit(solution)/shard_map/psum | solution.py:96
  1430.3 141.2 %all-reduce.21.cloned.1.call-done = f32[6,4096]{1,0:T(8,128)} async-done(((f32[6,4096]{1,0:T(8,128)}), f32[6,4096]{1,0:T(8,128)}) %all-reduce.21.cloned.1.call-update) | async-done | bytes 98320 | tf_op jit(solution)/shard_map/psum | solution.py:96
  1572.5 142.0 %all-reduce.23.cloned.1.call-done = f32[6,4096]{1,0:T(8,128)} async-done(((f32[6,4096]{1,0:T(8,128)}), f32[6,4096]{1,0:T(8,128)}) %all-reduce.23.cloned.1.call-update) | async-done | bytes 98320 | tf_op jit(solution)/shard_map/psum | solution.py:96
  (250 shorter events, 183.6 us)
Async XLA Ops:
  7.2 501.2 %all-reduce.9.cloned.1.call-start = ((), (), s32[]{:S(2)}) async-start(), calls=%async_computation | async-start | bytes 262144 | tf_op jit(solution)/shard_map/psum | solution.py:96
  78.7 11.5 copy-start.18
  289.1 0.6 copy-start.5
  289.8 357.4 %all-reduce.11.cloned.1.call-start = ((), (), s32[]{:S(2)}) async-start(), calls=%async_computation.1 | async-start | bytes 262144 | tf_op jit(solution)/shard_map/psum | solution.py:96
  327.5 2.3 copy-start.6
  362.7 0.7 copy-start.7
  396.2 100.8 %copy-start.8 = (f32[2,6,2048]{2,1,0:T(8,128)}, f32[2,6,2048]{2,1,0:T(8,128)S(1)}, u32[]{:S(2)}) copy-start(f32[2,6,2048]{2,1,0:T(8,128)S(1)} %get-tuple-element.238) | copy-start | bytes 294916
  397.6 543.1 %copy-start.15 = (s32[1024]{0:T(1024)}, s32[1024]{0:T(1024)S(1)}, u32[]{:S(2)}) copy-start(s32[1024]{0:T(1024)S(1)} %pad_clamp_fusion) | copy-start | bytes 12292
  399.7 99.4 %copy-start.11 = (f32[3,1024]{1,0:T(4,128)S(1)}, f32[3,1024]{1,0:T(4,128)}, u32[]{:S(2)}) copy-start(f32[3,1024]{1,0:T(4,128)} %param.23) | copy-start | bytes 36868
  399.7 99.6 %copy-start.12 = (f32[3,1024]{1,0:T(4,128)S(1)}, f32[3,1024]{1,0:T(4,128)}, u32[]{:S(2)}) copy-start(f32[3,1024]{1,0:T(4,128)} %param.25) | copy-start | bytes 36868
  399.7 99.8 %copy-start.13 = (f32[3,1024]{1,0:T(4,128)S(1)}, f32[3,1024]{1,0:T(4,128)}, u32[]{:S(2)}) copy-start(f32[3,1024]{1,0:T(4,128)} %param.24) | copy-start | bytes 36868
  399.7 100.7 %copy-start.14 = (f32[3,1024]{1,0:T(4,128)S(1)}, f32[3,1024]{1,0:T(4,128)}, u32[]{:S(2)}) copy-start(f32[3,1024]{1,0:T(4,128)} %param.26) | copy-start | bytes 36868
  508.4 281.0 %all-reduce.13.cloned.1.call-start = ((), (), s32[]{:S(2)}) async-start(), calls=%async_computation.2 | async-start | bytes 262144 | tf_op jit(solution)/shard_map/psum | solution.py:96
  647.2 285.0 %all-reduce.15.cloned.1.call-start = ((), (), s32[]{:S(2)}) async-start(), calls=%async_computation.3 | async-start | bytes 262144 | tf_op jit(solution)/shard_map/psum | solution.py:96
  789.4 497.1 %all-reduce.17.cloned.1.call-start = ((), (), s32[]{:S(2)}) async-start(), calls=%async_computation.4 | async-start | bytes 262144 | tf_op jit(solution)/shard_map/psum | solution.py:96
  934.7 74.5 %copy-start.2 = (f32[3,1024]{0,1:T(8,128)}, f32[3,1024]{0,1:T(8,128)S(1)}, u32[]{:S(2)}) copy-start(f32[3,1024]{0,1:T(8,128)S(1)} %scatter_fusion) | copy-start | bytes 36868
  936.3 73.0 %copy-start = (f32[3,1024]{0,1:T(8,128)}, f32[3,1024]{0,1:T(8,128)S(1)}, u32[]{:S(2)}) copy-start(f32[3,1024]{0,1:T(8,128)S(1)} %scatter_fusion.3) | copy-start | bytes 36868
  1110.7 2.9 copy-start.9
  1147.6 281.7 %all-reduce.19.cloned.1.call-start = ((), (), s32[]{:S(2)}) async-start(), calls=%async_computation.5 | async-start | bytes 262144 | tf_op jit(solution)/shard_map/psum | solution.py:96
  1183.0 0.7 copy-start.10
  1183.6 32.9 %copy-start.1 = (f32[3,1024]{0,1:T(8,128)S(1)}, f32[3,1024]{0,1:T(8,128)}, u32[]{:S(2)}) copy-start(f32[3,1024]{0,1:T(8,128)} %copy-done) | copy-start | bytes 36868
  1183.6 32.9 %copy-start.16 = (s32[1024]{0:T(1024)S(1)}, s32[1024]{0:T(1024)}, u32[]{:S(2)}) copy-start(s32[1024]{0:T(1024)} %copy-done.15) | copy-start | bytes 12292
  1183.6 34.3 %copy-start.3 = (f32[3,1024]{0,1:T(8,128)S(1)}, f32[3,1024]{0,1:T(8,128)}, u32[]{:S(2)}) copy-start(f32[3,1024]{0,1:T(8,128)} %copy-done.2) | copy-start | bytes 36868
  1183.6 531.7 %copy-start.19 = (f32[256]{0:T(256)S(1)}, f32[256]{0:T(256)}, u32[]{:S(2)}) copy-start(f32[256]{0:T(256)} %get-tuple-element.731) | copy-start | bytes 3076
  1183.6 531.7 %copy-start.20 = (f32[256]{0:T(256)S(1)}, f32[256]{0:T(256)}, u32[]{:S(2)}) copy-start(f32[256]{0:T(256)} %get-tuple-element.732) | copy-start | bytes 3076
  1183.7 531.9 %copy-start.17 = (s32[256,1]{0,1:T(1,128)S(1)}, s32[256,1]{0,1:T(1,128)}, u32[]{:S(2)}) copy-start(s32[256,1]{0,1:T(1,128)} %get-tuple-element.729) | copy-start | bytes 3076
  1216.5 355.0 %copy-start.4 = (f32[2,6,2048]{2,1,0:T(8,128)}, f32[2,6,2048]{2,1,0:T(8,128)S(1)}, u32[]{:S(2)}) copy-start(f32[2,6,2048]{2,1,0:T(8,128)S(1)} %get-tuple-element.248) | copy-start | bytes 294916
  1286.5 285.0 %all-reduce.21.cloned.1.call-start = ((), (), s32[]{:S(2)}) async-start(), calls=%async_computation.6 | async-start | bytes 262144 | tf_op jit(solution)/shard_map/psum | solution.py:96
  1429.3 285.1 %all-reduce.23.cloned.1.call-start = ((), (), s32[]{:S(2)}) async-start(), calls=%async_computation.7 | async-start | bytes 262144 | tf_op jit(solution)/shard_map/psum | solution.py:96
Sparse Core Ops, SparseCore 0:
  289.9 138.5 all-reduce.8
  508.5 138.5 all-reduce.10
  651.9 137.4 all-reduce.12
  794.7 137.4 all-reduce.14
  1147.8 138.6 all-reduce.16
  1291.8 137.4 all-reduce.18
  1434.0 137.4 all-reduce.20
  1577.0 137.4 all-reduce.22
where the time goes:
time: 1740 us; the launch traced here: 1730 us
  waiting for transfers between devices  913 us (52%)
  local copies, waits for them, and re-layouts  405 us (23%)
  other arithmetic  270 us (16%)
  blocking collectives  123 us (7%)
  between operations  19 us (1%)
    psum x8, waiting for transfers between devices, shards(): summed = lax.psum(terms, ('grp', 'dev'))  913 us
    reduce_sum x16, other arithmetic, pair_block(): jnp.sum(weight * (drift_z - along * gap_z), axis=1)  259 us
    gather x2, local copies, waits for them, and re-layouts, shards(): slot = owner * slot_cap + place - first[owner]  194 us
    all_gather x2, blocking collectives, shards(): gathered = lax.all_gather(targets[None], ('grp', 'dev'), axis=0, tiled=True)  123 us
    gather x2, local copies, waits for them, and re-layouts, shards(): compact = flat[:, slot]  120 us
  transfers between devices with their start and end apart: 8, of which 7 were waited for; matrix products, arithmetic and copies ran while one was open for 17% of the time, Pallas kernels for 0%

commit v1 on v0

--- a/solution.py
+++ b/solution.py
@@ -93,7 +93,7 @@
             if summed is not None:
                 terms, summed = lax.optimization_barrier((terms, summed))
                 parts.append(summed)
-            summed = lax.psum(terms, ("grp", "dev"))
+            summed = lax.psum(lax.psum(terms, "grp"), "dev")
         parts.append(summed)
         parts.append(jnp.zeros((6, slot_cap), jnp.float32))
         totals = jnp.concatenate(parts, axis=1)

time: 1740 us -> 1800 us (1.034)
  waiting for transfers between devices: 913 us -> 961 us
    psum x8 -> x16, waiting for transfers between devices: 913 us -> 961 us  [shards(): summed = lax.psum(lax.psum(terms, 'grp'), 'dev')]
  transfers between devices with their start and end apart: 8 -> 16, of which waited for: 7 -> 15; matrix products, arithmetic and copies ran while one was open for 17% -> 18% of each run, Pallas kernels for 0% -> 0%
where the time goes in v1:
time: 1800 us; the launch traced here: 1790 us
  waiting for transfers between devices  961 us (53%)
  local copies, waits for them, and re-layouts  408 us (23%)
  other arithmetic  274 us (15%)
  blocking collectives  125 us (7%)
  between operations  18.9 us (1%)
    psum x16, waiting for transfers between devices, shards(): summed = lax.psum(lax.psum(terms, 'grp'), 'dev')  961 us
    reduce_sum x16, other arithmetic, pair_block(): jnp.sum(weight * (drift_z - along * gap_z), axis=1)  262 us
    gather x2, local copies, waits for them, and re-layouts, shards(): slot = owner * slot_cap + place - first[owner]  194 us
    all_gather x2, blocking collectives, shards(): gathered = lax.all_gather(targets[None], ('grp', 'dev'), axis=0, tiled=True)  125 us
    gather x2, local copies, waits for them, and re-layouts, shards(): compact = flat[:, slot]  120 us
  transfers between devices with their start and end apart: 16, of which 15 were waited for; matrix products, arithmetic and copies ran while one was open for 18% of the time, Pallas kernels for 0%

profile of v1, /device:TPU:1, one launch (start us, length us, event | category | flops | bytes accessed | tf_op | source)
XLA Modules:
  0.0 1789.4 jit_solution(12625883050075476323)
XLA Ops:
  14.8 63.9 %all-gather.2 = f32[128,6,256]{2,1,0:T(8,128)S(1)} all-gather(f32[1,6,256]{2,1,0:T(8,128)S(1)} %maximum_bitcast_fusion), channel_id=2, replica_groups=mesh['grp'=8,'dev'=16] {'grp','dev'}, dimensions={0}, use_global_device_ids=true | all-gather | bytes 792576 | tf_op jit(solution)/shard_map/all_gather | solution.py:85
  90.3 97.2 %gather_fusion.6 = s32[16384]{0:T(1024)S(1)} fusion(s32[128]{0:T(128)S(1)} %get-tuple-element.734, s32[16384]{0:T(1024)S(1)} %broadcast_clamp_fusion.3), kind=kCustom, calls=%fused_computation.6 | custom fusion | bytes 196608 | tf_op jit(solution)/shard_map/gather | solution.py:84
  187.7 60.2 %gather_fusion.7 = f32[16384,6]{1,0:T(8,128)} fusion(f32[6,32768]{0,1:T(8,128)} %bitcast.632, s32[16384]{0:T(1024)S(1)} %broadcast_clamp_fusion.1), kind=kCustom, calls=%fused_computation.7 | custom fusion | bytes 851968 | tf_op jit(solution)/shard_map/gather | solution.py:87
  256.3 32.9 %while.81 = (s32[]{:T(128)}, f32[2,6,2048]{2,1,0:T(8,128)S(1)}, f32[3,1024]{1,0:T(4,128)S(1)}, f32[2,6,2048]{2,1,0:T(8,128)S(1)}, f32[3,1024]{1,0:T(4,128)S(1)},...) while((s32[]{:T(128)}, f32[2,6,2048]{2,1,0:T(8,128)S(1)}, ...), condition=%wide.region_17.18_spmd, body=%wide.region_10.17_spmd.sunk | while | flops 85970952 | bytes 499925 | solution.py:37
  294.9 32.9 %while.80 = (s32[]{:T(128)}, f32[2,6,2048]{2,1,0:T(8,128)S(1)}, f32[3,1024]{1,0:T(4,128)S(1)}, f32[2,6,2048]{2,1,0:T(8,128)S(1)}, f32[3,1024]{1,0:T(4,128)S(1)},...) while((s32[]{:T(128)}, f32[2,6,2048]{2,1,0:T(8,128)S(1)}, ...), condition=%wide.region_9.10_spmd, body=%wide.region_2.9_spmd.sunk | while | flops 85970952 | bytes 499925 | solution.py:37
  330.1 32.8 %while.82 = (s32[]{:T(128)}, f32[2,6,2048]{2,1,0:T(8,128)S(1)}, f32[3,1024]{1,0:T(4,128)S(1)}, f32[2,6,2048]{2,1,0:T(8,128)S(1)}, f32[3,1024]{1,0:T(4,128)S(1)},...) while((s32[]{:T(128)}, f32[2,6,2048]{2,1,0:T(8,128)S(1)}, ...), condition=%wide.region_27.28_spmd, body=%wide.region_20.27_spmd.sunk | while | flops 85970952 | bytes 499925 | solution.py:37
  363.6 32.8 %while.83 = (s32[]{:T(128)}, f32[2,6,2048]{2,1,0:T(8,128)S(1)}, f32[3,1024]{1,0:T(4,128)S(1)}, f32[2,6,2048]{2,1,0:T(8,128)S(1)}, f32[3,1024]{1,0:T(4,128)S(1)},...) while((s32[]{:T(128)}, f32[2,6,2048]{2,1,0:T(8,128)S(1)}, ...), condition=%wide.region_37.38_spmd, body=%wide.region_30.37_spmd.sunk | while | flops 85970952 | bytes 499925 | solution.py:37
  396.6 97.2 %gather_fusion.15 = s32[16384]{0:T(1024)S(1)} fusion(s32[128]{0:T(128)S(1)} %get-tuple-element.733, s32[16384]{0:T(1024)S(1)} %broadcast_clamp_fusion.2), kind=kCustom, calls=%fused_computation.15 | custom fusion | bytes 196608 | tf_op jit(solution)/shard_map/gather | solution.py:84
  496.9 76.3 %all-reduce.19.cloned.1.call-done = f32[6,4096]{1,0:T(8,128)} async-done(((f32[6,4096]{1,0:T(8,128)}), f32[6,4096]{1,0:T(8,128)}) %all-reduce.19.cloned.1.call-update) | async-done | bytes 98320 | tf_op jit(solution)/shard_map/psum | solution.py:96
  573.3 60.6 %all-reduce.21.cloned.1.call-done = f32[6,4096]{1,0:T(8,128)} async-done(((f32[6,4096]{1,0:T(8,128)}), f32[6,4096]{1,0:T(8,128)}) %all-reduce.21.cloned.1.call-update) | async-done | bytes 98320 | tf_op jit(solution)/shard_map/psum | solution.py:96
  633.9 84.8 %all-reduce.23.cloned.1.call-done = f32[6,4096]{1,0:T(8,128)} async-done(((f32[6,4096]{1,0:T(8,128)}), f32[6,4096]{1,0:T(8,128)}) %all-reduce.23.cloned.1.call-update) | async-done | bytes 98320 | tf_op jit(solution)/shard_map/psum | solution.py:96
  725.7 53.5 %all-reduce.25.cloned.1.call-done = f32[6,4096]{1,0:T(8,128)} async-done(((f32[6,4096]{1,0:T(8,128)}), f32[6,4096]{1,0:T(8,128)}) %all-reduce.25.cloned.1.call-update) | async-done | bytes 98320 | tf_op jit(solution)/shard_map/psum | solution.py:96
  780.2 83.9 %all-reduce.27.cloned.1.call-done = f32[6,4096]{1,0:T(8,128)} async-done(((f32[6,4096]{1,0:T(8,128)}), f32[6,4096]{1,0:T(8,128)}) %all-reduce.27.cloned.1.call-update) | async-done | bytes 98320 | tf_op jit(solution)/shard_map/psum | solution.py:96
  865.1 59.7 %all-reduce.29.cloned.1.call-done = f32[6,4096]{1,0:T(8,128)} async-done(((f32[6,4096]{1,0:T(8,128)}), f32[6,4096]{1,0:T(8,128)}) %all-reduce.29.cloned.1.call-update) | async-done | bytes 98320 | tf_op jit(solution)/shard_map/psum | solution.py:96
  925.7 84.0 %all-reduce.31.cloned.1.call-done = f32[6,4096]{1,0:T(8,128)} async-done(((f32[6,4096]{1,0:T(8,128)}), f32[6,4096]{1,0:T(8,128)}) %all-reduce.31.cloned.1.call-update) | async-done | bytes 98320 | tf_op jit(solution)/shard_map/psum | solution.py:96
  1019.4 60.8 %all-gather.3 = f32[128,6,256]{2,1,0:T(8,128)S(1)} all-gather(f32[1,6,256]{2,1,0:T(8,128)S(1)} %maximum_bitcast_fusion.1), channel_id=3, replica_groups=mesh['grp'=8,'dev'=16] {'grp','dev'}, dimensions={0}, use_global_device_ids=true | all-gather | bytes 792576 | tf_op jit(solution)/shard_map/all_gather | solution.py:85
  1088.5 60.2 %gather_fusion.16 = f32[16384,6]{1,0:T(8,128)} fusion(f32[6,32768]{0,1:T(8,128)} %bitcast.633, s32[16384]{0:T(1024)S(1)} %broadcast_clamp_fusion), kind=kCustom, calls=%fused_computation.16 | custom fusion | bytes 851968 | tf_op jit(solution)/shard_map/gather | solution.py:87
  1157.1 35.4 %while.85 = (s32[]{:T(128)}, f32[2,6,2048]{2,1,0:T(8,128)S(1)}, f32[3,1024]{1,0:T(4,128)S(1)}, f32[2,6,2048]{2,1,0:T(8,128)S(1)}, f32[3,1024]{1,0:T(4,128)S(1)},...) while((s32[]{:T(128)}, f32[2,6,2048]{2,1,0:T(8,128)S(1)}, ...), condition=%wide.region_64.65_spmd, body=%wide.region_57.64_spmd.sunk | while | flops 85970952 | bytes 499925 | solution.py:37
  1174.9 16.8 fusion.195
  1197.5 51.5 %all-reduce.33.cloned.1.call-done = f32[6,4096]{1,0:T(8,128)} async-done(((f32[6,4096]{1,0:T(8,128)}), f32[6,4096]{1,0:T(8,128)}) %all-reduce.33.cloned.1.call-update) | async-done | bytes 98320 | tf_op jit(solution)/shard_map/psum | solution.py:96
  1249.3 35.4 %while.84 = (s32[]{:T(128)}, f32[2,6,2048]{2,1,0:T(8,128)S(1)}, f32[3,1024]{1,0:T(4,128)S(1)}, f32[2,6,2048]{2,1,0:T(8,128)S(1)}, f32[3,1024]{1,0:T(4,128)S(1)},...) while((s32[]{:T(128)}, f32[2,6,2048]{2,1,0:T(8,128)S(1)}, ...), condition=%wide.region_56.57_spmd, body=%wide.region_49.56_spmd.sunk | while | flops 85970952 | bytes 499925 | solution.py:37
  1249.4 16.8 fusion.193
  1267.2 16.8 fusion.193
  1284.8 49.1 %all-reduce.35.cloned.1.call-done = f32[6,4096]{1,0:T(8,128)} async-done(((f32[6,4096]{1,0:T(8,128)}), f32[6,4096]{1,0:T(8,128)}) %all-reduce.35.cloned.1.call-update) | async-done | bytes 98320 | tf_op jit(solution)/shard_map/psum | solution.py:96
  1340.0 54.6 %all-reduce.37.cloned.1.call-done = f32[6,4096]{1,0:T(8,128)} async-done(((f32[6,4096]{1,0:T(8,128)}), f32[6,4096]{1,0:T(8,128)}) %all-reduce.37.cloned.1.call-update) | async-done | bytes 98320 | tf_op jit(solution)/shard_map/psum | solution.py:96
  1394.6 32.9 %while.86 = (s32[]{:T(128)}, f32[2,6,2048]{2,1,0:T(8,128)S(1)}, f32[3,1024]{1,0:T(4,128)S(1)}, f32[2,6,2048]{2,1,0:T(8,128)S(1)}, f32[3,1024]{1,0:T(4,128)S(1)},...) while((s32[]{:T(128)}, f32[2,6,2048]{2,1,0:T(8,128)S(1)}, ...), condition=%wide.region_74.75_spmd, body=%wide.region_67.74_spmd.sunk | while | flops 85970952 | bytes 499925 | solution.py:37
  1428.1 51.3 %all-reduce.39.cloned.1.call-done = f32[6,4096]{1,0:T(8,128)} async-done(((f32[6,4096]{1,0:T(8,128)}), f32[6,4096]{1,0:T(8,128)}) %all-reduce.39.cloned.1.call-update) | async-done | bytes 98320 | tf_op jit(solution)/shard_map/psum | solution.py:96
  1479.6 32.9 %while.87 = (s32[]{:T(128)}, f32[2,6,2048]{2,1,0:T(8,128)S(1)}, f32[3,1024]{1,0:T(4,128)S(1)}, f32[2,6,2048]{2,1,0:T(8,128)S(1)}, f32[3,1024]{1,0:T(4,128)S(1)},...) while((s32[]{:T(128)}, f32[2,6,2048]{2,1,0:T(8,128)S(1)}, ...), condition=%wide.region_84.85_spmd, body=%wide.region_77.84_spmd.sunk | while | flops 85970952 | bytes 499925 | solution.py:37
  1515.8 24.3 %all-reduce.41.cloned.1.call-done = f32[6,4096]{1,0:T(8,128)} async-done(((f32[6,4096]{1,0:T(8,128)}), f32[6,4096]{1,0:T(8,128)}) %all-reduce.41.cloned.1.call-update) | async-done | bytes 98320 | tf_op jit(solution)/shard_map/psum | solution.py:96
  1540.8 84.1 %all-reduce.43.cloned.1.call-done = f32[6,4096]{1,0:T(8,128)} async-done(((f32[6,4096]{1,0:T(8,128)}), f32[6,4096]{1,0:T(8,128)}) %all-reduce.43.cloned.1.call-update) | async-done | bytes 98320 | tf_op jit(solution)/shard_map/psum | solution.py:96
  1625.7 59.7 %all-reduce.45.cloned.1.call-done = f32[6,4096]{1,0:T(8,128)} async-done(((f32[6,4096]{1,0:T(8,128)}), f32[6,4096]{1,0:T(8,128)}) %all-reduce.45.cloned.1.call-update) | async-done | bytes 98320 | tf_op jit(solution)/shard_map/psum | solution.py:96
  1687.0 83.3 %all-reduce.47.cloned.1.call-done = f32[6,4096]{1,0:T(8,128)} async-done(((f32[6,4096]{1,0:T(8,128)}), f32[6,4096]{1,0:T(8,128)}) %all-reduce.47.cloned.1.call-update) | async-done | bytes 98320 | tf_op jit(solution)/shard_map/psum | solution.py:96
  (280 shorter events, 319.2 us)
Async XLA Ops:
  7.2 486.8 %all-reduce.17.cloned.1.call-start = ((), (), s32[]{:S(2)}) async-start(), calls=%async_computation | async-start | bytes 262144 | tf_op jit(solution)/shard_map/psum | solution.py:96
  289.8 283.4 %all-reduce.19.cloned.1.call-start = ((), (), s32[]{:S(2)}) async-start(), calls=%async_computation.1 | async-start | bytes 262144 | tf_op jit(solution)/shard_map/psum | solution.py:96
  396.4 97.4 %copy-start.8 = (f32[2,6,2048]{2,1,0:T(8,128)}, f32[2,6,2048]{2,1,0:T(8,128)S(1)}, u32[]{:S(2)}) copy-start(f32[2,6,2048]{2,1,0:T(8,128)S(1)} %get-tuple-element.238) | copy-start | bytes 294916
  396.6 322.4 %copy-start.14 = (f32[3,1024]{1,0:T(4,128)S(1)}, f32[3,1024]{1,0:T(4,128)}, u32[]{:S(2)}) copy-start(f32[3,1024]{1,0:T(4,128)} %param.23) | copy-start | bytes 36868
  396.6 322.6 %copy-start.15 = (f32[3,1024]{1,0:T(4,128)S(1)}, f32[3,1024]{1,0:T(4,128)}, u32[]{:S(2)}) copy-start(f32[3,1024]{1,0:T(4,128)} %param.25) | copy-start | bytes 36868
  396.6 322.9 %copy-start.16 = (f32[3,1024]{1,0:T(4,128)S(1)}, f32[3,1024]{1,0:T(4,128)}, u32[]{:S(2)}) copy-start(f32[3,1024]{1,0:T(4,128)} %param.24) | copy-start | bytes 36868
  396.6 323.7 %copy-start.17 = (f32[3,1024]{1,0:T(4,128)S(1)}, f32[3,1024]{1,0:T(4,128)}, u32[]{:S(2)}) copy-start(f32[3,1024]{1,0:T(4,128)} %param.26) | copy-start | bytes 36868
  494.0 139.8 %all-reduce.21.cloned.1.call-start = ((), (), s32[]{:S(2)}) async-start(), calls=%async_computation.2 | async-start | bytes 262144 | tf_op jit(solution)/shard_map/psum | solution.py:96
  573.2 145.5 %all-reduce.23.cloned.1.call-start = ((), (), s32[]{:S(2)}) async-start(), calls=%async_computation.3 | async-start | bytes 262144 | tf_op jit(solution)/shard_map/psum | solution.py:96
  633.9 145.3 %all-reduce.25.cloned.1.call-start = ((), (), s32[]{:S(2)}) async-start(), calls=%async_computation.4 | async-start | bytes 262144 | tf_op jit(solution)/shard_map/psum | solution.py:96
  718.7 145.3 %all-reduce.27.cloned.1.call-start = ((), (), s32[]{:S(2)}) async-start(), calls=%async_computation.5 | async-start | bytes 262144 | tf_op jit(solution)/shard_map/psum | solution.py:96
  719.0 300.3 %copy-start.18 = (s32[1024]{0:T(1024)}, s32[1024]{0:T(1024)S(1)}, u32[]{:S(2)}) copy-start(s32[1024]{0:T(1024)S(1)} %pad_clamp_fusion) | copy-start | bytes 12292
  779.2 145.5 %all-reduce.29.cloned.1.call-start = ((), (), s32[]{:S(2)}) async-start(), calls=%async_computation.6 | async-start | bytes 262144 | tf_op jit(solution)/shard_map/psum | solution.py:96
  864.1 145.6 %all-reduce.31.cloned.1.call-start = ((), (), s32[]{:S(2)}) async-start(), calls=%async_computation.7 | async-start | bytes 262144 | tf_op jit(solution)/shard_map/psum | solution.py:96
  924.7 324.3 %all-reduce.33.cloned.1.call-start = ((), (), s32[]{:S(2)}) async-start(), calls=%async_computation.8 | async-start | bytes 262144 | tf_op jit(solution)/shard_map/psum | solution.py:96
  1012.3 76.3 %copy-start.2 = (f32[3,1024]{0,1:T(8,128)}, f32[3,1024]{0,1:T(8,128)S(1)}, u32[]{:S(2)}) copy-start(f32[3,1024]{0,1:T(8,128)S(1)} %scatter_fusion) | copy-start | bytes 36868
  1013.8 74.7 %copy-start = (f32[3,1024]{0,1:T(8,128)}, f32[3,1024]{0,1:T(8,128)S(1)}, u32[]{:S(2)}) copy-start(f32[3,1024]{0,1:T(8,128)S(1)} %scatter_fusion.3) | copy-start | bytes 36868
  1193.2 140.7 %all-reduce.35.cloned.1.call-start = ((), (), s32[]{:S(2)}) async-start(), calls=%async_computation.9 | async-start | bytes 262144 | tf_op jit(solution)/shard_map/psum | solution.py:96
  1249.1 145.5 %all-reduce.37.cloned.1.call-start = ((), (), s32[]{:S(2)}) async-start(), calls=%async_computation.10 | async-start | bytes 262144 | tf_op jit(solution)/shard_map/psum | solution.py:96
  1284.8 49.1 %copy-start.10 = (f32[2,6,2048]{2,1,0:T(8,128)}, f32[2,6,2048]{2,1,0:T(8,128)S(1)}, u32[]{:S(2)}) copy-start(f32[2,6,2048]{2,1,0:T(8,128)S(1)} %get-tuple-element.242) | copy-start | bytes 294916
  1333.9 145.5 %all-reduce.39.cloned.1.call-start = ((), (), s32[]{:S(2)}) async-start(), calls=%async_computation.11 | async-start | bytes 262144 | tf_op jit(solution)/shard_map/psum | solution.py:96
  1394.6 145.5 %all-reduce.41.cloned.1.call-start = ((), (), s32[]{:S(2)}) async-start(), calls=%async_computation.12 | async-start | bytes 262144 | tf_op jit(solution)/shard_map/psum | solution.py:96
  1427.5 51.9 %copy-start.11 = (f32[2,6,2048]{2,1,0:T(8,128)}, f32[2,6,2048]{2,1,0:T(8,128)S(1)}, u32[]{:S(2)}) copy-start(f32[2,6,2048]{2,1,0:T(8,128)S(1)} %get-tuple-element.245) | copy-start | bytes 294916
  1479.5 145.5 %all-reduce.43.cloned.1.call-start = ((), (), s32[]{:S(2)}) async-start(), calls=%async_computation.13 | async-start | bytes 262144 | tf_op jit(solution)/shard_map/psum | solution.py:96
  1479.5 60.6 %copy-start.12 = (f32[6,4096]{1,0:T(8,128)S(1)}, f32[6,4096]{1,0:T(8,128)}, u32[]{:S(2)}) copy-start(f32[6,4096]{1,0:T(8,128)} %all-reduce.35.cloned.1.call-done) | copy-start | bytes 294916
  1479.6 145.5 %copy-start.13 = (f32[6,4096]{1,0:T(8,128)S(1)}, f32[6,4096]{1,0:T(8,128)}, u32[]{:S(2)}) copy-start(f32[6,4096]{1,0:T(8,128)} %all-reduce.39.cloned.1.call-done) | copy-start | bytes 294916
  1479.6 292.9 %copy-start.22 = (f32[256]{0:T(256)S(1)}, f32[256]{0:T(256)}, u32[]{:S(2)}) copy-start(f32[256]{0:T(256)} %get-tuple-element.731) | copy-start | bytes 3076
  1479.6 292.9 %copy-start.23 = (f32[256]{0:T(256)S(1)}, f32[256]{0:T(256)}, u32[]{:S(2)}) copy-start(f32[256]{0:T(256)} %get-tuple-element.732) | copy-start | bytes 3076
  1479.6 293.9 %copy-start.20 = (s32[256,1]{0,1:T(1,128)S(1)}, s32[256,1]{0,1:T(1,128)}, u32[]{:S(2)}) copy-start(s32[256,1]{0,1:T(1,128)} %get-tuple-element.729) | copy-start | bytes 3076
  1512.5 112.4 %copy-start.4 = (f32[2,6,2048]{2,1,0:T(8,128)}, f32[2,6,2048]{2,1,0:T(8,128)S(1)}, u32[]{:S(2)}) copy-start(f32[2,6,2048]{2,1,0:T(8,128)S(1)} %get-tuple-element.248) | copy-start | bytes 294916
  1540.1 145.3 %all-reduce.45.cloned.1.call-start = ((), (), s32[]{:S(2)}) async-start(), calls=%async_computation.14 | async-start | bytes 262144 | tf_op jit(solution)/shard_map/psum | solution.py:96
  1625.0 145.3 %all-reduce.47.cloned.1.call-start = ((), (), s32[]{:S(2)}) async-start(), calls=%async_computation.15 | async-start | bytes 262144 | tf_op jit(solution)/shard_map/psum | solution.py:96
  (8 other events, 116.1 us)
Sparse Core Ops, SparseCore 0:
  289.9 55.8 all-reduce.16
  494.1 78.9 all-reduce.18
  575.5 58.2 all-reduce.20
  637.2 81.4 all-reduce.22
  720.9 58.2 all-reduce.24
  782.6 81.4 all-reduce.26
  866.4 58.2 all-reduce.28
  928.2 81.4 all-reduce.30
  1193.3 55.6 all-reduce.32
  1252.4 81.4 all-reduce.34
  1336.2 58.2 all-reduce.36
  1397.9 81.4 all-reduce.38
  1481.7 58.2 all-reduce.40
  1543.4 81.4 all-reduce.42
  1627.1 58.2 all-reduce.44
  1688.8 81.4 all-reduce.46
